TPU v7x, 256 devices: a whole 4x4x8 slice. The times are simulated.
256 devices in a mesh: ctx: 16 (over z, x_hi), head: 16 (over x_lo, y, core).
Axes of the slice: x: 4 (x_hi: 2, x_lo: 2; x = x_hi * 2 + x_lo), y: 4, z: 8, core: 2. Of those that a mesh axis runs over, the one named last changes fastest.
Arguments:
- queries: bfloat16 [16384, 8192], P('ctx', 'head'), may hold values from -5.5 to 5.5
- keys: bfloat16 [16384, 512], P(('ctx', 'head')), may hold values from -5.5 to 5.5
- values: bfloat16 [16384, 512], P(('ctx', 'head')), may hold values from -6 to 6
- comp_k_weight: float32 [32, 512], replicated, may hold values from -0.79549513 to 0.79549513
- comp_v_weight: float32 [32, 512], replicated, may hold values from -1 to 1
- gate_logits: float32 [3, 64, 16384], P(None, 'head', 'ctx'), may hold values from -6 to 6
- sel_tiles: int32 [64, 64], replicated, may hold values from 0 to 243, as said below
Outputs:
- attended: bfloat16 [16384, 8192], P('ctx', 'head')
Inputs may be any that keep to these rules, and one draw needn't show every extreme that they name: `sel_tiles`: among the indices of the query blocks of one ctx shard (4 blocks) for one group, exactly 2 distinct tiles lie in each ctx shard up to and including their own and none in later ones; the first index of every query block names a tile among the first 4 tiles of its own ctx shard; indices may repeat within a block.
All inputs are finite; a program needn't handle non-finite values.
Results may differ from a plain program's by a relative error of at most 0.012.
Values may be sent and summed in bfloat16 or wider, within the bound.
No kernel may reach another device: no remote copies, remote signals or barrier semaphores. Data moves between devices by JAX's collectives and lax.ppermute only.
A program may use at most 64 MiB of HBM per device.

v0:
```python
import jax
import jax.numpy as jnp
from jax import lax
from jax.sharding import PartitionSpec as P

H = 64
G = 4
HD = 128
KERN = 32
STRIDE = 16
TILE = 64
TOPK = 16
WIN = 512
QB = 256
CAP = 2


def shifted(block, axis, distance):
    devices = range(lax.axis_size(axis))
    route = [(i - distance, i) for i in devices if i - distance in devices]
    return lax.ppermute(block, axis, route)


def online_step(folded, query_head, block_kv, allowed):
    running_max, running_sum, accum_out = folded
    scores = jnp.einsum(
        "qd,kd->qk", query_head, block_kv[:, :HD], preferred_element_type=jnp.float32
    ) * HD ** (-0.5)
    block_peak = jnp.max(jnp.where(allowed, scores, -jnp.inf), axis=-1)
    fresh_max = jnp.maximum(running_max, block_peak)
    weights = jnp.where(allowed, jnp.exp(scores - fresh_max[:, None]), 0.0)
    shrink = jnp.exp(running_max - fresh_max)
    running_sum = running_sum * shrink + jnp.sum(weights, axis=-1)
    product = jnp.dot(
        weights.astype(jnp.bfloat16), block_kv[:, HD:], preferred_element_type=jnp.float32
    )
    accum_out = accum_out * shrink[:, None] + product
    return (fresh_max, running_sum, accum_out)


def heads_step(folded, query_heads, block_kv, allowed):

    def per_head(element):
        return online_step((element[0], element[1], element[2]), element[3], block_kv, allowed)

    return lax.map(per_head, (folded[0], folded[1], folded[2], query_heads))


def finish(folded):
    return folded[2] / folded[1][..., None]


def local(queries, keys, values, comp_k_weight, comp_v_weight, gate_logits, sel_tiles):
    ctx_count = lax.axis_size("ctx")
    ctx_index = lax.axis_index("ctx")
    head_index = lax.axis_index("head")
    local_rows = queries.shape[0]
    local_heads = queries.shape[1] // HD
    group_index = head_index * local_heads // (H // G)
    all_keys, all_values = (
        lax.all_gather(keys, "head", axis=0, tiled=True),
        lax.all_gather(values, "head", axis=0, tiled=True),
    )
    group_keys = lax.dynamic_slice_in_dim(all_keys, group_index * HD, HD, 1)
    group_values = lax.dynamic_slice_in_dim(all_values, group_index * HD, HD, 1)
    group_kv = jnp.concatenate([group_keys, group_values], axis=1)
    positions = ctx_index * local_rows + jnp.arange(local_rows)
    query_heads = queries.reshape(local_rows, local_heads, HD).transpose(1, 0, 2)
    tail_rows = shifted(group_kv[: KERN - STRIDE], "ctx", -1)
    extended = jnp.concatenate([group_kv, tail_rows], axis=0)
    comp_weight = jnp.concatenate(
        [
            lax.dynamic_slice_in_dim(comp_k_weight, group_index * HD, HD, 1),
            lax.dynamic_slice_in_dim(comp_v_weight, group_index * HD, HD, 1),
        ],
        axis=1,
    )
    comp_local = local_rows // STRIDE
    first_half = extended[:local_rows].reshape(comp_local, STRIDE, 2 * HD).astype(jnp.float32)
    second_half = (
        extended[STRIDE : STRIDE + local_rows]
        .reshape(comp_local, STRIDE, 2 * HD)
        .astype(jnp.float32)
    )
    compressed = (
        jnp.sum(first_half * comp_weight[None, :STRIDE], 1)
        + jnp.sum(second_half * comp_weight[None, STRIDE:], 1)
    ).astype(jnp.bfloat16)
    sink_init = (
        jnp.zeros((local_heads, local_rows), jnp.float32),
        jnp.ones((local_heads, local_rows), jnp.float32),
        jnp.zeros((local_heads, local_rows, HD), jnp.float32),
    )
    shard_rows = lax.all_gather(compressed, "ctx", axis=0, tiled=True)
    row_count = shard_rows.shape[0]
    wide_block = min(row_count, 512)
    grouped = shard_rows.reshape(row_count // wide_block, wide_block, 2 * HD)

    def scan_step(running, element):
        block_kv, block_index = element
        block_end = (block_index * wide_block + jnp.arange(wide_block)) * STRIDE + KERN - 1
        allowed = block_end[None, :] <= positions[:, None]
        return (heads_step(running, query_heads, block_kv, allowed), None)

    result, unused = lax.scan(scan_step, sink_init, (grouped, jnp.arange(row_count // wide_block)))
    comp_out = finish(result)
    previous = shifted(group_kv[local_rows - WIN :], "ctx", 1)
    window_kv = jnp.concatenate([previous, group_kv], axis=0)

    def window_block(block_index):
        row_begin = block_index * WIN
        query_part = lax.dynamic_slice_in_dim(query_heads, row_begin, WIN, 1)
        kv_part = lax.dynamic_slice_in_dim(window_kv, row_begin, 2 * WIN, 0)
        key_pos = ctx_index * local_rows + row_begin - WIN + jnp.arange(2 * WIN)
        query_pos = ctx_index * local_rows + row_begin + jnp.arange(WIN)
        allowed = (
            (key_pos[None, :] <= query_pos[:, None])
            & (key_pos[None, :] > query_pos[:, None] - WIN)
            & (key_pos[None, :] >= 0)
        )
        window_init = (
            jnp.full((local_heads, WIN), -jnp.inf, jnp.float32),
            jnp.zeros((local_heads, WIN), jnp.float32),
            jnp.zeros((local_heads, WIN, HD), jnp.float32),
        )
        return finish(heads_step(window_init, query_part, kv_part, allowed))

    win_blocks = lax.map(window_block, jnp.arange(local_rows // WIN))
    win_out = win_blocks.transpose(1, 0, 2, 3).reshape(local_heads, local_rows, HD)
    block_count = local_rows // QB
    tiles_shard = local_rows // TILE
    group_tiles = lax.dynamic_slice_in_dim(sel_tiles, group_index * TOPK, TOPK, 1)
    own_tiles = lax.dynamic_slice_in_dim(group_tiles, ctx_index * block_count, block_count, 0)
    own_flat = own_tiles.reshape(-1)
    query_blocks = query_heads.reshape(local_heads, block_count, QB, HD).transpose(1, 0, 2, 3)
    sel_init = (
        jnp.zeros((block_count, local_heads, QB), jnp.float32),
        jnp.ones((block_count, local_heads, QB), jnp.float32),
        jnp.zeros((block_count, local_heads, QB, HD), jnp.float32),
    )
    requests = group_tiles.reshape(ctx_count, block_count * TOPK)
    local_ids = ctx_index * tiles_shard + jnp.arange(tiles_shard)
    present = jnp.any(requests[:, :, None] == local_ids[None, None, :], axis=1)
    order_rank = jnp.cumsum(present.astype(jnp.int32), axis=1) - 1
    picked = present[:, None, :] & (order_rank[:, None, :] == jnp.arange(CAP)[None, :, None])
    outbox = jnp.einsum(
        "dct,tx->dcx",
        picked.astype(jnp.bfloat16),
        group_kv.reshape(tiles_shard, TILE * 2 * HD),
        preferred_element_type=jnp.float32,
    ).astype(jnp.bfloat16)
    received = lax.all_to_all(outbox, "ctx", split_axis=0, concat_axis=0, tiled=True)
    all_ids = jnp.arange(ctx_count * tiles_shard).reshape(ctx_count, tiles_shard)
    wanted = jnp.any(own_flat[:, None, None] == all_ids[None, :, :], axis=0)
    wanted_rank = jnp.cumsum(wanted.astype(jnp.int32), axis=1) - 1
    chosen = wanted[:, None, :] & (wanted_rank[:, None, :] == jnp.arange(CAP)[None, :, None])
    slot_tile = jnp.sum(jnp.where(chosen, all_ids[:, None, :], 0), axis=2).reshape(-1)
    slot_ok = jnp.any(chosen, axis=2).reshape(-1)
    slot_kv = received.reshape(ctx_count * CAP * TILE, 2 * HD)
    key_pos = (slot_tile[:, None] * TILE + jnp.arange(TILE)[None, :]).reshape(-1)

    def per_block(element):
        block_max, block_sum, block_out, block_query, block_tiles, block_index = element
        is_named = slot_ok & jnp.any(block_tiles[:, None] == slot_tile[None, :], axis=0)
        key_ok = jnp.repeat(is_named, TILE)
        query_pos = ctx_index * local_rows + block_index * QB + jnp.arange(QB)
        allowed = key_ok[None, :] & (key_pos[None, :] <= query_pos[:, None])
        return heads_step((block_max, block_sum, block_out), block_query, slot_kv, allowed)

    sel_state = lax.map(
        per_block,
        (sel_init[0], sel_init[1], sel_init[2], query_blocks, own_tiles, jnp.arange(block_count)),
    )
    sel_out = finish(sel_state).transpose(1, 0, 2, 3).reshape(local_heads, local_rows, HD)
    gate_values = jax.nn.sigmoid(gate_logits)
    combined = (
        gate_values[0][..., None] * comp_out
        + gate_values[1][..., None] * sel_out
        + gate_values[2][..., None] * win_out
    )
    return combined.transpose(1, 0, 2).reshape(local_rows, local_heads * HD).astype(jnp.bfloat16)


def solution(mesh):
    placed = (
        P("ctx", "head"),
        P(("ctx", "head"), None),
        P(("ctx", "head"), None),
        P(),
        P(),
        P(None, "head", "ctx"),
        P(),
    )
    return jax.shard_map(
        local, mesh=mesh, in_specs=placed, out_specs=P("ctx", "head"), check_vma=False
    )
```

profile of v0, /device:TPU:6, one launch (start us, length us, event | category | flops | bytes accessed | tf_op | source)
XLA Modules:
  0.0 365.0 jit_solution(1468088390830321323)
XLA Ops:
  16.6 30.0 %all-gather.5.cloned.1.call-done = bf16[1024,512]{1,0:T(8,128)(2,1)} async-done(((bf16[64,512]{1,0:T(8,128)(2,1)}), bf16[1024,512]{1,0:T(8,128)(2,1)}) %all-gather.5.cloned.1.call-update) | async-done | bytes 1048592 | tf_op jit(solution)/shard_map/all_gather | solution.py:62
  47.7 35.7 %all-gather.3.cloned.1.call-done = bf16[1024,512]{1,0:T(8,128)(2,1)} async-done(((bf16[64,512]{1,0:T(8,128)(2,1)}), bf16[1024,512]{1,0:T(8,128)(2,1)}) %all-gather.3.cloned.1.call-update) | async-done | bytes 1048592 | tf_op jit(solution)/shard_map/all_gather | solution.py:61
  84.9 3.2 collective-permute-start
  89.2 2.1 copy.45
  91.2 10.0 %all-to-all-start = ((bf16[16,2,16384]{2,1,0:T(2,128)(2,1)}), bf16[16,2,16384]{2,1,0:T(2,128)(2,1)}, u32[]{:S(2)}, u32[]{:S(2)}) async-start(bf16[16,2,16384]{2,1,0:T(2,128)(2,1)} %copy.45), calls=%async_computation | async-start | bytes 2097152 | tf_op jit(solution)/shard_map/all_to_all | solution.py:152
  101.2 3.4 collective-permute-start.1
  104.9 60.8 %all_gather.11 = bf16[1024,256]{1,0:T(8,128)(2,1)S(1)} all-gather(bf16[64,256]{1,0:T(8,128)(2,1)S(1)} %add_convert_fusion), channel_id=1, replica_groups=mesh['ctx'=16,'head'=16] {'ctx'}, dimensions={0}, use_global_device_ids=true | all-gather | bytes 557056 | tf_op jit(solution)/shard_map/all_gather | solution.py:94
  167.1 40.8 %while.135 = (s32[]{:T(128)}, f32[4,1024]{1,0:T(4,128)S(1)}, f32[4,1024]{1,0:T(4,128)S(1)}, f32[4,1024,128]{2,1,0:T(8,128)}, bf16[2,512,256]{2,1,0:T(8,128)(2,1)...) while((s32[]{:T(128)}, f32[4,1024]{1,0:T(4,128)S(1)}, ...), condition=%wide.region_7.8_spmd.clone, body=%wide.region_2.7_spmd.clone.sunk | while | flops 276044288 | bytes 9548170 | solution.py:105
  168.5 19.0 %while.139 = (s32[]{:T(128)}, f32[4,1024]{1,0:T(4,128)S(1)}, f32[4,1024]{1,0:T(4,128)S(1)}, f32[4,1024,128]{2,1,0:T(8,128)}, bf16[4,1024,128]{2,1,0:T(8,128)(2,1...) while((s32[]{:T(128)}, f32[4,1024]{1,0:T(4,128)S(1)}, ...), condition=%wide.region_6.6_spmd.clone.clone, body=%wide.region_3.5_spmd.clone.clone.sunk | while | flops 276041728 | bytes 9017481 | solution.py:46
  188.9 19.0 %while.139 = (s32[]{:T(128)}, f32[4,1024]{1,0:T(4,128)S(1)}, f32[4,1024]{1,0:T(4,128)S(1)}, f32[4,1024,128]{2,1,0:T(8,128)}, bf16[4,1024,128]{2,1,0:T(8,128)(2,1...) while((s32[]{:T(128)}, f32[4,1024]{1,0:T(4,128)S(1)}, ...), condition=%wide.region_6.6_spmd.clone.clone, body=%wide.region_3.5_spmd.clone.clone.sunk | while | flops 276041728 | bytes 9017481 | solution.py:46
  209.0 49.2 %while.133 = (s32[]{:T(128)}, f32[2,4,512,128]{3,2,1,0:T(8,128)}, s32[2]{0:T(128)S(1)}, bf16[4,1024,128]{2,1,0:T(8,128)(2,1)}, bf16[1536,256]{1,0:T(8,128)(2,1)S...) while((s32[]{:T(128)}, f32[2,4,512,128]{3,2,1,0:T(8,128)}, ...), condition=%wide.region_26.27_spmd, body=%wide.region_21.26_spmd.sunk | while | flops 280826368 | bytes 17762856 | solution.py:128
  210.3 1.9 constant_dynamic-slice_fusion.14
  213.0 19.2 %while.138 = (s32[]{:T(128)}, f32[4,512]{1,0:T(4,128)S(1)}, f32[4,512,128]{2,1,0:T(8,128)S(1)}, bf16[4,512,128]{2,1,0:T(8,128)(2,1)}, bf16[1024,256]{1,0:T(8,128...) while((s32[]{:T(128)}, f32[4,512]{1,0:T(4,128)S(1)}, ...), condition=%wide.region_25.25_spmd.clone, body=%wide.region_22.24_spmd.clone.sunk | while | flops 280560128 | bytes 7259265 | solution.py:46
  213.0 1.8 select_reduce_fusion.6
  216.0 1.9 fusion.107
  217.8 1.8 select_reduce_fusion.6
  220.8 1.9 fusion.107
  222.7 1.8 select_reduce_fusion.6
  225.6 1.9 fusion.107
  227.5 1.9 select_reduce_fusion.6
  230.4 1.9 fusion.107
  234.8 1.9 constant_dynamic-slice_fusion.14
  237.6 19.2 %while.138 = (s32[]{:T(128)}, f32[4,512]{1,0:T(4,128)S(1)}, f32[4,512,128]{2,1,0:T(8,128)S(1)}, bf16[4,512,128]{2,1,0:T(8,128)(2,1)}, bf16[1024,256]{1,0:T(8,128...) while((s32[]{:T(128)}, f32[4,512]{1,0:T(4,128)S(1)}, ...), condition=%wide.region_25.25_spmd.clone, body=%wide.region_22.24_spmd.clone.sunk | while | flops 280560128 | bytes 7259265 | solution.py:46
  237.6 1.8 select_reduce_fusion.6
  240.5 1.9 fusion.107
  242.4 1.9 select_reduce_fusion.6
  245.4 1.9 fusion.107
  247.2 1.8 select_reduce_fusion.6
  250.2 1.9 fusion.107
  252.0 1.9 select_reduce_fusion.6
  255.0 1.9 fusion.107
  258.2 3.1 copy.52
  261.3 2.5 reshape.241
  263.9 86.8 %while.137 = (s32[]{:T(128)}, f32[4,4,256]{2,0,1:T(4,128)S(1)}, f32[4,4,256,128]{3,2,0,1:T(8,128)}, bf16[4,4,256,128]{3,2,0,1:T(8,128)(2,1)}, s32[4,16]{1,0:T(4,...) while((s32[]{:T(128)}, f32[4,4,256]{2,0,1:T(4,128)S(1)}, ...), condition=%wide.wide.region_20.21_spmd.clone, body=%wide.wide.region_14.20_spmd.clone.sunk | while | flops 276336640 | bytes 9205774 | solution.py:170
  267.2 17.5 %while.140 = (s32[]{:T(128)}, f32[4,256]{1,0:T(4,128)S(1)}, f32[4,256,128]{2,1,0:T(8,128)S(1)}, bf16[4,256,128]{2,1,0:T(8,128)(2,1)S(1)}, bf16[2048,256]{1,0:T(8...) while((s32[]{:T(128)}, f32[4,256]{1,0:T(4,128)S(1)}, ...), condition=%wide.region_19.19_spmd.clone, body=%wide.region_16.18_spmd.clone.sunk | while | flops 276333312 | bytes 7583865 | solution.py:46
  269.8 1.8 fusion.98
  274.1 1.8 fusion.98
  275.9 1.7 select_reduce_fusion.5
  278.5 1.8 fusion.98
  280.3 1.7 select_reduce_fusion.5
  282.9 1.8 fusion.98
  288.9 17.5 %while.140 = (s32[]{:T(128)}, f32[4,256]{1,0:T(4,128)S(1)}, f32[4,256,128]{2,1,0:T(8,128)S(1)}, bf16[4,256,128]{2,1,0:T(8,128)(2,1)S(1)}, bf16[2048,256]{1,0:T(8...) while((s32[]{:T(128)}, f32[4,256]{1,0:T(4,128)S(1)}, ...), condition=%wide.region_19.19_spmd.clone, body=%wide.region_16.18_spmd.clone.sunk | while | flops 276333312 | bytes 7583865 | solution.py:46
  291.4 1.8 fusion.98
  293.2 1.7 select_reduce_fusion.5
  295.8 1.8 fusion.98
  300.2 1.8 fusion.98
  302.0 1.7 select_reduce_fusion.5
  304.6 1.8 fusion.98
  310.5 17.5 %while.140 = (s32[]{:T(128)}, f32[4,256]{1,0:T(4,128)S(1)}, f32[4,256,128]{2,1,0:T(8,128)S(1)}, bf16[4,256,128]{2,1,0:T(8,128)(2,1)S(1)}, bf16[2048,256]{1,0:T(8...) while((s32[]{:T(128)}, f32[4,256]{1,0:T(4,128)S(1)}, ...), condition=%wide.region_19.19_spmd.clone, body=%wide.region_16.18_spmd.clone.sunk | while | flops 276333312 | bytes 7583865 | solution.py:46
  313.1 1.8 fusion.98
  314.9 1.7 select_reduce_fusion.5
  317.5 1.8 fusion.98
  319.3 1.7 select_reduce_fusion.5
  321.9 1.8 fusion.98
  323.7 1.7 select_reduce_fusion.5
  326.2 1.8 fusion.98
  332.2 17.5 %while.140 = (s32[]{:T(128)}, f32[4,256]{1,0:T(4,128)S(1)}, f32[4,256,128]{2,1,0:T(8,128)S(1)}, bf16[4,256,128]{2,1,0:T(8,128)(2,1)S(1)}, bf16[2048,256]{1,0:T(8...) while((s32[]{:T(128)}, f32[4,256]{1,0:T(4,128)S(1)}, ...), condition=%wide.region_19.19_spmd.clone, body=%wide.region_16.18_spmd.clone.sunk | while | flops 276333312 | bytes 7583865 | solution.py:46
  334.8 1.8 fusion.98
  339.2 1.8 fusion.98
  341.0 1.7 select_reduce_fusion.5
  343.5 1.8 fusion.98
  347.9 1.8 fusion.98
  350.7 2.1 broadcast_divide_fusion
  353.5 2.8 fusion.64
  (347 shorter events, 113.3 us)
Async XLA Ops:
  6.5 40.1 %all-gather.5.cloned.1.call-start = ((), (), s32[]{:S(2)}) async-start(), calls=%async_computation.2 | async-start | bytes 1114112 | tf_op jit(solution)/shard_map/all_gather | solution.py:62
  7.3 76.1 %all-gather.3.cloned.1.call-start = ((), (), s32[]{:S(2)}) async-start(), calls=%async_computation.1 | async-start | bytes 1114112 | tf_op jit(solution)/shard_map/all_gather | solution.py:61
  8.1 2.8 copy-start.10
  8.1 7.9 %copy-start.9 = (f32[3,4,1024]{2,1,0:T(4,128)S(1)}, f32[3,4,1024]{2,1,0:T(4,128)}, u32[]{:S(2)}) copy-start(f32[3,4,1024]{2,1,0:T(4,128)} %param.24) | copy-start | bytes 147460
  11.0 0.5 copy-start.14
  12.4 2.9 copy-start.11
  84.9 19.7 %collective-permute-start = (bf16[16,256]{1,0:T(8,128)(2,1)S(1)}, bf16[16,256]{1,0:T(8,128)(2,1)S(1)}, u32[]{:S(2)}, u32[]{:S(2)}) collective-permute-start(bf16[16,256]{1,0:T(8,128)(2,1)S(1)} %fusion.73), channel_id=1, source_target_pairs={{16,0},{32,16},{48,32},{64,48},{80,64},{96,80},{112,96},{128,112},... | collective-permute-start | bytes 24584 | tf_op jit(solution)/shard_map/ppermute | solution.py:21
  91.2 170.1 %all-to-all-start = ((bf16[16,2,16384]{2,1,0:T(2,128)(2,1)}), bf16[16,2,16384]{2,1,0:T(2,128)(2,1)}, u32[]{:S(2)}, u32[]{:S(2)}) async-start(bf16[16,2,16384]{2,1,0:T(2,128)(2,1)} %copy.45), calls=%async_computation | async-start | bytes 2097152 | tf_op jit(solution)/shard_map/all_to_all | solution.py:152
  101.2 106.7 %collective-permute-start.1 = (bf16[512,256]{1,0:T(8,128)(2,1)}, bf16[512,256]{1,0:T(8,128)(2,1)}, u32[]{:S(2)}, u32[]{:S(2)}) collective-permute-start(bf16[512,256]{1,0:T(8,128)(2,1)} %fusion.67), channel_id=1, source_target_pairs={{0,16},{16,32},{32,48},{48,64},{64,80},{80,96},{96,112},{112,128},... | collective-permute-start | bytes 786440 | tf_op jit(solution)/shard_map/ppermute | solution.py:21
  207.9 1.1 copy-start.4
  209.0 4.0 %copy-start.1 = (bf16[1536,256]{1,0:T(8,128)(2,1)}, bf16[1536,256]{1,0:T(8,128)(2,1)S(1)}, u32[]{:S(2)}) copy-start(bf16[1536,256]{1,0:T(8,128)(2,1)S(1)} %get-tuple-element.1592) | copy-start | bytes 2359300 | tf_op jit(solution)/shard_map/while
  232.3 1.4 copy-start.2
  233.6 4.0 %copy-start.1 = (bf16[1536,256]{1,0:T(8,128)(2,1)}, bf16[1536,256]{1,0:T(8,128)(2,1)S(1)}, u32[]{:S(2)}) copy-start(bf16[1536,256]{1,0:T(8,128)(2,1)S(1)} %get-tuple-element.1592) | copy-start | bytes 2359300 | tf_op jit(solution)/shard_map/while
  256.9 1.3 copy-start.2
  261.3 2.6 copy-start.12
  261.3 2.6 copy-start.13
  261.3 2.6 copy-start.15
  261.3 2.6 copy-start.16
  263.8 88.9 %copy-start.6 = (f32[4,1024]{1,0:T(4,128)S(1)}, f32[4,1024]{1,0:T(4,128)}, u32[]{:S(2)}) copy-start(f32[4,1024]{1,0:T(4,128)} %get-tuple-element.952) | copy-start | bytes 49156
  263.9 88.9 %copy-start.7 = (f32[4,1024]{1,0:T(4,128)S(1)}, f32[4,1024]{1,0:T(4,128)}, u32[]{:S(2)}) copy-start(f32[4,1024]{1,0:T(4,128)} %get-tuple-element.953) | copy-start | bytes 49156
  263.9 88.9 %copy-start.8 = (f32[4,1024]{1,0:T(4,128)S(1)}, f32[4,1024]{1,0:T(4,128)}, u32[]{:S(2)}) copy-start(f32[4,1024]{1,0:T(4,128)} %get-tuple-element.954) | copy-start | bytes 49156
  350.6 2.2 copy-start
  350.7 2.9 copy-start.3
  350.7 2.9 copy-start.5
Sparse Core Ops, SparseCore 0:
  9.2 37.4 all-gather.4
  48.5 34.7 all-gather.2
where the time goes:
time: 368 us; the launch traced here: 365 us
  matrix products  110 us (30%)
  waiting for transfers between devices  67.1 us (18%)
  blocking collectives  60.8 us (17%)
  local copies, waits for them, and re-layouts  53.5 us (15%)
  other arithmetic  37 us (10%)
  starting transfers between devices  16.6 us (5%)
  between operations  13.7 us (4%)
  loops' own time  6.32 us (2%)
    all_gather x1, blocking collectives, local(): shard_rows = lax.all_gather(compressed, 'ctx', axis=0, tiled=True)  60.8 us
    dot_general x32, matrix products, online_step(): jnp.dot(weights.astype(jnp.bfloat16), block_kv[:, HD:], preferred_element...  55.7 us
    dot_general x32, matrix products, online_step(): jnp.einsum('qd,kd->qk', query_head, block_kv[:, :HD], preferred_element_t...  53.9 us
    all_gather x1, waiting for transfers between devices, local(): lax.all_gather(keys, 'head', axis=0, tiled=True)  35.7 us
    all_gather x1, waiting for transfers between devices, local(): lax.all_gather(values, 'head', axis=0, tiled=True)  30 us
    reduce_sum x32, other arithmetic, online_step(): running_sum = running_sum * shrink + jnp.sum(weights, axis=-1)  24.2 us
    all_to_all x1, starting transfers between devices, local(): lax.all_to_all(outbox, 'ctx', split_axis=0, concat_axis=0, tiled=True)  9.99 us
    dynamic_slice x16, local copies, waits for them, and re-layouts, heads_step(): return lax.map(per_head, (folded[0], folded[1], folded[2], query_heads))  8.75 us
  transfers between devices with their start and end apart: 5, of which 2 were waited for; matrix products, arithmetic and copies ran while one was open for 29% of the time, Pallas kernels for 0%

commit v1 on v0

--- a/solution.py
+++ b/solution.py
@@ -1,3 +1,4 @@
+import functools
 import jax
 import jax.numpy as jnp
 from jax import lax
@@ -13,6 +14,15 @@
 WIN = 512
 QB = 256
 CAP = 2
+
+
+def take_area(inp, across, dim_at):
+    g_now = jnp.stack([inp for _ in range(jax.lax.axis_size(across))])
+    found_now = jax.lax.all_to_all(g_now, across, 0, 0)
+    return jnp.concatenate(found_now, axis=dim_at)
+
+
+_measure_domain = functools.partial(take_area, across="head", dim_at=0)
 
 
 def shifted(block, axis, distance):
@@ -58,7 +68,7 @@
     local_heads = queries.shape[1] // HD
     group_index = head_index * local_heads // (H // G)
     all_keys, all_values = (
-        lax.all_gather(keys, "head", axis=0, tiled=True),
+        _measure_domain(keys),
         lax.all_gather(values, "head", axis=0, tiled=True),
     )
     group_keys = lax.dynamic_slice_in_dim(all_keys, group_index * HD, HD, 1)

time: 368 us -> 335 us (0.910)
  waiting for transfers between devices: 67.1 us -> 26.9 us
  starting transfers between devices: 16.6 us -> 23.4 us
    all_gather x1 -> x0, waiting for transfers between devices: 35.7 us -> none  [local(): lax.all_gather(keys, 'head', axis=0, tiled=True)]
    all_gather x1, waiting for transfers between devices: 30 us -> 17.4 us  [local(): lax.all_gather(values, 'head', axis=0, tiled=True)]
    all_to_all x0 -> x1, waiting for transfers between devices: none -> 8.79 us  [take_area(): found_now = jax.lax.all_to_all(g_now, across, 0, 0)]
    all_to_all x0 -> x1, starting transfers between devices: none -> 5.95 us  [take_area(): found_now = jax.lax.all_to_all(g_now, across, 0, 0)]
  transfers between devices with their start and end apart: 5 -> 5, of which waited for: 2 -> 2; matrix products, arithmetic and copies ran while one was open for 29% -> 32% of each run, Pallas kernels for 0% -> 0%
where the time goes in v1:
time: 335 us; the launch traced here: 332 us
  matrix products  110 us (33%)
  blocking collectives  60.8 us (18%)
  local copies, waits for them, and re-layouts  53.5 us (16%)
  other arithmetic  37 us (11%)
  waiting for transfers between devices  26.9 us (8%)
  starting transfers between devices  23.4 us (7%)
  between operations  13.7 us (4%)
  loops' own time  6.32 us (2%)
    all_gather x1, blocking collectives, local(): shard_rows = lax.all_gather(compressed, 'ctx', axis=0, tiled=True)  60.8 us
    dot_general x32, matrix products, online_step(): jnp.dot(weights.astype(jnp.bfloat16), block_kv[:, HD:], preferred_element...  55.7 us
    dot_general x32, matrix products, online_step(): jnp.einsum('qd,kd->qk', query_head, block_kv[:, :HD], preferred_element_t...  54 us
    reduce_sum x32, other arithmetic, online_step(): running_sum = running_sum * shrink + jnp.sum(weights, axis=-1)  24.2 us
    all_gather x1, waiting for transfers between devices, local(): lax.all_gather(values, 'head', axis=0, tiled=True)  17.4 us
    all_to_all x1, starting transfers between devices, local(): lax.all_to_all(outbox, 'ctx', split_axis=0, concat_axis=0, tiled=True)  10.8 us
    all_to_all x1, waiting for transfers between devices, take_area(): found_now = jax.lax.all_to_all(g_now, across, 0, 0)  8.79 us
    dynamic_slice x16, local copies, waits for them, and re-layouts, heads_step(): return lax.map(per_head, (folded[0], folded[1], folded[2], query_heads))  8.75 us
  transfers between devices with their start and end apart: 5, of which 2 were waited for; matrix products, arithmetic and copies ran while one was open for 32% of the time, Pallas kernels for 0%

profile of v1, /device:TPU:6, one launch (start us, length us, event | category | flops | bytes accessed | tf_op | source)
XLA Modules:
  0.0 331.7 jit_solution(16600755621538105065)
XLA Ops:
  7.3 2.0 stack.2
  9.2 5.9 %all-to-all-start = ((bf16[16,64,512]{2,1,0:T(8,128)(2,1)}), bf16[16,64,512]{2,1,0:T(8,128)(2,1)S(1)}, u32[]{:S(2)}, u32[]{:S(2)}) async-start(bf16[16,64,512]{2,1,0:T(8,128)(2,1)} %stack.2), calls=%async_computation | async-start | bytes 2097152 | tf_op jit(solution)/shard_map/all_to_all | solution.py:21
  22.8 8.8 %all-to-all-done = bf16[16,64,512]{2,1,0:T(8,128)(2,1)S(1)} async-done(((bf16[16,64,512]{2,1,0:T(8,128)(2,1)}), bf16[16,64,512]{2,1,0:T(8,128)(2,1)S(1)}, u32[]{:S(2)}, u32[]{:S(2)}) %all-to-all-start) | async-done | bytes 1048608 | tf_op jit(solution)/shard_map/all_to_all | solution.py:21
  31.7 17.4 %all-gather.2.cloned.1.call-done = bf16[1024,512]{1,0:T(8,128)(2,1)} async-done(((bf16[64,512]{1,0:T(8,128)(2,1)}), bf16[1024,512]{1,0:T(8,128)(2,1)}) %all-gather.2.cloned.1.call-update) | async-done | bytes 1048592 | tf_op jit(solution)/shard_map/all_gather | solution.py:72
  50.6 3.3 %collective-permute-start = (bf16[16,256]{1,0:T(8,128)(2,1)S(1)}, bf16[16,256]{1,0:T(8,128)(2,1)S(1)}, u32[]{:S(2)}, u32[]{:S(2)}) collective-permute-start(bf16[16,256]{1,0:T(8,128)(2,1)S(1)} %fusion.73), channel_id=1, source_target_pairs={{16,0},{32,16},{48,32},{64,48},{80,64},{96,80},{112,96},{128,112},... | collective-permute-start | bytes 24584 | tf_op jit(solution)/shard_map/ppermute | solution.py:31
  55.0 2.1 copy.45
  57.1 10.8 %all-to-all-start.1 = ((bf16[16,2,16384]{2,1,0:T(2,128)(2,1)}), bf16[16,2,16384]{2,1,0:T(2,128)(2,1)}, u32[]{:S(2)}, u32[]{:S(2)}) async-start(bf16[16,2,16384]{2,1,0:T(2,128)(2,1)} %copy.45), calls=%async_computation.1 | async-start | bytes 2097152 | tf_op jit(solution)/shard_map/all_to_all | solution.py:162
  67.9 3.4 %collective-permute-start.1 = (bf16[512,256]{1,0:T(8,128)(2,1)}, bf16[512,256]{1,0:T(8,128)(2,1)}, u32[]{:S(2)}, u32[]{:S(2)}) collective-permute-start(bf16[512,256]{1,0:T(8,128)(2,1)} %fusion.67), channel_id=1, source_target_pairs={{0,16},{16,32},{32,48},{48,64},{64,80},{80,96},{96,112},{112,128},... | collective-permute-start | bytes 786440 | tf_op jit(solution)/shard_map/ppermute | solution.py:31
  71.5 60.8 %all_gather.7 = bf16[1024,256]{1,0:T(8,128)(2,1)S(1)} all-gather(bf16[64,256]{1,0:T(8,128)(2,1)S(1)} %add_convert_fusion), channel_id=1, replica_groups=mesh['ctx'=16,'head'=16] {'ctx'}, dimensions={0}, use_global_device_ids=true | all-gather | bytes 557056 | tf_op jit(solution)/shard_map/all_gather | solution.py:104
  133.8 40.8 %while.135 = (s32[]{:T(128)}, f32[4,1024]{1,0:T(4,128)S(1)}, f32[4,1024]{1,0:T(4,128)S(1)}, f32[4,1024,128]{2,1,0:T(8,128)}, bf16[2,512,256]{2,1,0:T(8,128)(2,1)...) while((s32[]{:T(128)}, f32[4,1024]{1,0:T(4,128)S(1)}, ...), condition=%wide.region_7.8_spmd.clone, body=%wide.region_2.7_spmd.clone.sunk | while | flops 276044288 | bytes 9548170 | solution.py:115
  135.1 19.0 %while.139 = (s32[]{:T(128)}, f32[4,1024]{1,0:T(4,128)S(1)}, f32[4,1024]{1,0:T(4,128)S(1)}, f32[4,1024,128]{2,1,0:T(8,128)}, bf16[4,1024,128]{2,1,0:T(8,128)(2,1...) while((s32[]{:T(128)}, f32[4,1024]{1,0:T(4,128)S(1)}, ...), condition=%wide.region_6.6_spmd.clone.clone, body=%wide.region_3.5_spmd.clone.clone.sunk | while | flops 276041728 | bytes 9017481 | solution.py:56
  155.5 19.0 %while.139 = (s32[]{:T(128)}, f32[4,1024]{1,0:T(4,128)S(1)}, f32[4,1024]{1,0:T(4,128)S(1)}, f32[4,1024,128]{2,1,0:T(8,128)}, bf16[4,1024,128]{2,1,0:T(8,128)(2,1...) while((s32[]{:T(128)}, f32[4,1024]{1,0:T(4,128)S(1)}, ...), condition=%wide.region_6.6_spmd.clone.clone, body=%wide.region_3.5_spmd.clone.clone.sunk | while | flops 276041728 | bytes 9017481 | solution.py:56
  175.6 49.2 %while.133 = (s32[]{:T(128)}, f32[2,4,512,128]{3,2,1,0:T(8,128)}, s32[2]{0:T(128)S(1)}, bf16[4,1024,128]{2,1,0:T(8,128)(2,1)}, bf16[1536,256]{1,0:T(8,128)(2,1)S...) while((s32[]{:T(128)}, f32[2,4,512,128]{3,2,1,0:T(8,128)}, ...), condition=%wide.region_26.27_spmd, body=%wide.region_21.26_spmd.sunk | while | flops 280826368 | bytes 17762856 | solution.py:138
  176.9 1.9 constant_dynamic-slice_fusion.14
  179.7 19.2 %while.138 = (s32[]{:T(128)}, f32[4,512]{1,0:T(4,128)S(1)}, f32[4,512,128]{2,1,0:T(8,128)S(1)}, bf16[4,512,128]{2,1,0:T(8,128)(2,1)}, bf16[1024,256]{1,0:T(8,128...) while((s32[]{:T(128)}, f32[4,512]{1,0:T(4,128)S(1)}, ...), condition=%wide.region_25.25_spmd.clone, body=%wide.region_22.24_spmd.clone.sunk | while | flops 280560128 | bytes 7259265 | solution.py:56
  179.7 1.9 select_reduce_fusion.6
  182.6 1.9 fusion.107
  184.5 1.8 select_reduce_fusion.6
  187.4 1.9 fusion.107
  189.3 1.9 select_reduce_fusion.6
  192.2 1.9 fusion.107
  194.1 1.8 select_reduce_fusion.6
  197.0 1.9 fusion.107
  201.5 1.9 constant_dynamic-slice_fusion.14
  204.3 19.2 %while.138 = (s32[]{:T(128)}, f32[4,512]{1,0:T(4,128)S(1)}, f32[4,512,128]{2,1,0:T(8,128)S(1)}, bf16[4,512,128]{2,1,0:T(8,128)(2,1)}, bf16[1024,256]{1,0:T(8,128...) while((s32[]{:T(128)}, f32[4,512]{1,0:T(4,128)S(1)}, ...), condition=%wide.region_25.25_spmd.clone, body=%wide.region_22.24_spmd.clone.sunk | while | flops 280560128 | bytes 7259265 | solution.py:56
  204.3 1.8 select_reduce_fusion.6
  207.2 1.9 fusion.107
  209.1 1.9 select_reduce_fusion.6
  212.0 1.9 fusion.107
  213.9 1.8 select_reduce_fusion.6
  216.8 1.9 fusion.107
  218.7 1.9 select_reduce_fusion.6
  221.6 1.9 fusion.107
  224.9 3.1 copy.52
  227.9 2.5 reshape.247
  230.5 86.8 %while.137 = (s32[]{:T(128)}, f32[4,4,256]{2,0,1:T(4,128)S(1)}, f32[4,4,256,128]{3,2,0,1:T(8,128)}, bf16[4,4,256,128]{3,2,0,1:T(8,128)(2,1)}, s32[4,16]{1,0:T(4,...) while((s32[]{:T(128)}, f32[4,4,256]{2,0,1:T(4,128)S(1)}, ...), condition=%wide.wide.region_20.21_spmd.clone, body=%wide.wide.region_14.20_spmd.clone.sunk | while | flops 276336640 | bytes 9205774 | solution.py:180
  233.8 17.5 %while.140 = (s32[]{:T(128)}, f32[4,256]{1,0:T(4,128)S(1)}, f32[4,256,128]{2,1,0:T(8,128)S(1)}, bf16[4,256,128]{2,1,0:T(8,128)(2,1)S(1)}, bf16[2048,256]{1,0:T(8...) while((s32[]{:T(128)}, f32[4,256]{1,0:T(4,128)S(1)}, ...), condition=%wide.region_19.19_spmd.clone, body=%wide.region_16.18_spmd.clone.sunk | while | flops 276333312 | bytes 7583865 | solution.py:56
  236.4 1.8 fusion.98
  240.8 1.8 fusion.98
  242.6 1.7 select_reduce_fusion.5
  245.2 1.8 fusion.98
  247.0 1.7 select_reduce_fusion.5
  249.5 1.8 fusion.98
  255.5 17.5 %while.140 = (s32[]{:T(128)}, f32[4,256]{1,0:T(4,128)S(1)}, f32[4,256,128]{2,1,0:T(8,128)S(1)}, bf16[4,256,128]{2,1,0:T(8,128)(2,1)S(1)}, bf16[2048,256]{1,0:T(8...) while((s32[]{:T(128)}, f32[4,256]{1,0:T(4,128)S(1)}, ...), condition=%wide.region_19.19_spmd.clone, body=%wide.region_16.18_spmd.clone.sunk | while | flops 276333312 | bytes 7583865 | solution.py:56
  258.1 1.8 fusion.98
  262.5 1.8 fusion.98
  266.8 1.8 fusion.98
  268.7 1.7 select_reduce_fusion.5
  271.2 1.8 fusion.98
  277.2 17.5 %while.140 = (s32[]{:T(128)}, f32[4,256]{1,0:T(4,128)S(1)}, f32[4,256,128]{2,1,0:T(8,128)S(1)}, bf16[4,256,128]{2,1,0:T(8,128)(2,1)S(1)}, bf16[2048,256]{1,0:T(8...) while((s32[]{:T(128)}, f32[4,256]{1,0:T(4,128)S(1)}, ...), condition=%wide.region_19.19_spmd.clone, body=%wide.region_16.18_spmd.clone.sunk | while | flops 276333312 | bytes 7583865 | solution.py:56
  279.8 1.8 fusion.98
  281.6 1.7 select_reduce_fusion.5
  284.2 1.8 fusion.98
  288.5 1.8 fusion.98
  290.3 1.7 select_reduce_fusion.5
  292.9 1.8 fusion.98
  298.9 17.5 %while.140 = (s32[]{:T(128)}, f32[4,256]{1,0:T(4,128)S(1)}, f32[4,256,128]{2,1,0:T(8,128)S(1)}, bf16[4,256,128]{2,1,0:T(8,128)(2,1)S(1)}, bf16[2048,256]{1,0:T(8...) while((s32[]{:T(128)}, f32[4,256]{1,0:T(4,128)S(1)}, ...), condition=%wide.region_19.19_spmd.clone, body=%wide.region_16.18_spmd.clone.sunk | while | flops 276333312 | bytes 7583865 | solution.py:56
  301.4 1.8 fusion.98
  305.8 1.8 fusion.98
  307.6 1.7 select_reduce_fusion.5
  310.2 1.8 fusion.98
  314.6 1.8 fusion.98
  317.3 2.1 broadcast_divide_fusion
  320.2 2.8 fusion.64
  (349 shorter events, 114.2 us)
Async XLA Ops:
  6.5 8.7 %copy-start.6 = (bf16[1024,512]{1,0:T(8,128)(2,1)S(1)}, bf16[1024,512]{1,0:T(8,128)(2,1)}, u32[]{:S(2)}) copy-start(bf16[1024,512]{1,0:T(8,128)(2,1)} %param.19) | copy-start | bytes 3145732
  6.5 42.5 %all-gather.2.cloned.1.call-start = ((), (), s32[]{:S(2)}) async-start(), calls=%async_computation.2 | async-start | bytes 1114112 | tf_op jit(solution)/shard_map/all_gather | solution.py:72
  9.2 22.4 %all-to-all-start = ((bf16[16,64,512]{2,1,0:T(8,128)(2,1)}), bf16[16,64,512]{2,1,0:T(8,128)(2,1)S(1)}, u32[]{:S(2)}, u32[]{:S(2)}) async-start(bf16[16,64,512]{2,1,0:T(8,128)(2,1)} %stack.2), calls=%async_computation | async-start | bytes 2097152 | tf_op jit(solution)/shard_map/all_to_all | solution.py:21
  15.2 1.9 copy-start.11
  15.2 6.9 %copy-start.10 = (f32[3,4,1024]{2,1,0:T(4,128)S(1)}, f32[3,4,1024]{2,1,0:T(4,128)}, u32[]{:S(2)}) copy-start(f32[3,4,1024]{2,1,0:T(4,128)} %param.24) | copy-start | bytes 147460
  17.2 0.5 copy-start.15
  18.5 31.8 %copy-start.12 = (s32[16,2]{1,0:T(8,128)}, s32[16,2]{1,0:T(8,128)S(1)}, u32[]{:S(2)}) copy-start(s32[16,2]{1,0:T(8,128)S(1)} %copy.48) | copy-start | bytes 388
  50.6 20.6 %collective-permute-start = (bf16[16,256]{1,0:T(8,128)(2,1)S(1)}, bf16[16,256]{1,0:T(8,128)(2,1)S(1)}, u32[]{:S(2)}, u32[]{:S(2)}) collective-permute-start(bf16[16,256]{1,0:T(8,128)(2,1)S(1)} %fusion.73), channel_id=1, source_target_pairs={{16,0},{32,16},{48,32},{64,48},{80,64},{96,80},{112,96},{128,112},... | collective-permute-start | bytes 24584 | tf_op jit(solution)/shard_map/ppermute | solution.py:31
  57.1 170.8 %all-to-all-start.1 = ((bf16[16,2,16384]{2,1,0:T(2,128)(2,1)}), bf16[16,2,16384]{2,1,0:T(2,128)(2,1)}, u32[]{:S(2)}, u32[]{:S(2)}) async-start(bf16[16,2,16384]{2,1,0:T(2,128)(2,1)} %copy.45), calls=%async_computation.1 | async-start | bytes 2097152 | tf_op jit(solution)/shard_map/all_to_all | solution.py:162
  67.9 106.7 %collective-permute-start.1 = (bf16[512,256]{1,0:T(8,128)(2,1)}, bf16[512,256]{1,0:T(8,128)(2,1)}, u32[]{:S(2)}, u32[]{:S(2)}) collective-permute-start(bf16[512,256]{1,0:T(8,128)(2,1)} %fusion.67), channel_id=1, source_target_pairs={{0,16},{16,32},{32,48},{48,64},{64,80},{80,96},{96,112},{112,128},... | collective-permute-start | bytes 786440 | tf_op jit(solution)/shard_map/ppermute | solution.py:31
  174.6 1.1 copy-start.4
  175.6 4.0 %copy-start.1 = (bf16[1536,256]{1,0:T(8,128)(2,1)}, bf16[1536,256]{1,0:T(8,128)(2,1)S(1)}, u32[]{:S(2)}) copy-start(bf16[1536,256]{1,0:T(8,128)(2,1)S(1)} %get-tuple-element.1592) | copy-start | bytes 2359300 | tf_op jit(solution)/shard_map/while
  198.9 1.4 copy-start.2
  200.3 4.0 %copy-start.1 = (bf16[1536,256]{1,0:T(8,128)(2,1)}, bf16[1536,256]{1,0:T(8,128)(2,1)S(1)}, u32[]{:S(2)}) copy-start(bf16[1536,256]{1,0:T(8,128)(2,1)S(1)} %get-tuple-element.1592) | copy-start | bytes 2359300 | tf_op jit(solution)/shard_map/while
  223.5 1.3 copy-start.2
  227.9 2.6 copy-start.13
  227.9 2.6 copy-start.14
  227.9 2.6 copy-start.16
  227.9 2.6 copy-start.17
  230.5 88.9 %copy-start.7 = (f32[4,1024]{1,0:T(4,128)S(1)}, f32[4,1024]{1,0:T(4,128)}, u32[]{:S(2)}) copy-start(f32[4,1024]{1,0:T(4,128)} %get-tuple-element.952) | copy-start | bytes 49156
  230.5 88.9 %copy-start.8 = (f32[4,1024]{1,0:T(4,128)S(1)}, f32[4,1024]{1,0:T(4,128)}, u32[]{:S(2)}) copy-start(f32[4,1024]{1,0:T(4,128)} %get-tuple-element.953) | copy-start | bytes 49156
  230.5 88.9 %copy-start.9 = (f32[4,1024]{1,0:T(4,128)S(1)}, f32[4,1024]{1,0:T(4,128)}, u32[]{:S(2)}) copy-start(f32[4,1024]{1,0:T(4,128)} %get-tuple-element.954) | copy-start | bytes 49156
  317.3 2.2 copy-start
  317.3 2.9 copy-start.3
  317.3 2.9 copy-start.5
Sparse Core Ops, SparseCore 0:
  9.2 39.7 all-gather.1
